TPU v7x, 32 devices: a whole 2x2x4 slice. The times are simulated.
32 devices in a mesh: seq: 8 (over y, x, core), head: 4 (over z).
Axes of the slice: x: 2, y: 2, z: 4, core: 2. Of those that a mesh axis runs over, the one named last changes fastest.
Arguments:
- queries: bfloat16 [4096, 64, 128], P(('seq', 'head')), may hold values from -36 to 36
- keys: bfloat16 [4096, 8, 128], P(('seq', 'head')), may hold values from -6 to 6
- values: bfloat16 [4096, 8, 128], P(('seq', 'head')), may hold values from -6 to 6
- output_gradient: bfloat16 [4096, 64, 128], P(('seq', 'head')), may hold values from -6 to 6
- global_blocks: int32 [2], replicated, may hold values from 0 to 31, as said below
- random_blocks: int32 [32, 3], replicated, may hold values from 0 to 31, as said below
Outputs:
- out: bfloat16 [4096, 64, 128], P(('seq', 'head'))
- grad_queries: bfloat16 [4096, 64, 128], P(('seq', 'head'))
- grad_keys: bfloat16 [4096, 8, 128], P(('seq', 'head'))
- grad_values: bfloat16 [4096, 8, 128], P(('seq', 'head'))
Inputs may be any that keep to these rules, and one draw needn't show every extreme that they name: `global_blocks`: the two blocks differ; one of them is the last block, 31. `random_blocks`: call 4 consecutive blocks starting at a multiple of 4 a group. The entries listed by a group's query blocks never lie in that group's own blocks, and at most 2 of them lie in any one other group; in every group some other group is hit exactly 2 times.
All inputs are finite; a program needn't handle non-finite values.
Results may differ from a plain program's by a relative error of at most 0.035.
Values may be sent and summed in bfloat16 or wider, within the bound.
No kernel may reach another device: no remote copies, remote signals or barrier semaphores. Data moves between devices by JAX's collectives and lax.ppermute only.
A program may use at most 128 MiB of HBM per device.

v0:
```python
import math
import jax
import jax.numpy as jnp
from jax import lax
from jax.sharding import PartitionSpec as P

BLOCK_TOKENS = 128


def padded(shard, sides, width):
    for axis, dim in sides:
        count, length = (lax.axis_size(axis), shard.shape[dim])
        up = [(i, (i + 1) % count) for i in range(count - 1)]
        down = [(j, i) for i, j in up]
        last = lax.slice_in_dim(shard, length - width, length, axis=dim)
        leading = lax.slice_in_dim(shard, 0, width, axis=dim)
        before = lax.ppermute(last, axis, up)
        after = lax.ppermute(leading, axis, down)
        shard = jnp.concatenate([before, shard, after], axis=dim)
    return shard


def from_root(block, axis, owner):
    block = jnp.where(lax.axis_index(axis) == owner, block, jnp.zeros_like(block))
    return lax.psum(block, axis)


def tree_sum(part, axis):
    count = lax.axis_size(axis)
    if count & count - 1:
        return lax.psum(part.astype(jnp.bfloat16), axis).astype(jnp.float32)
    stride = 1
    while stride < count:
        pairs = [(i, i ^ stride) for i in range(count)]
        other = lax.ppermute(part.astype(jnp.bfloat16), axis, pairs)
        part = part + other.astype(jnp.float32)
        stride *= 2
    return part


def head_exchange(array, split_axis, concat_axis):
    count = lax.axis_size("head")
    own = lax.axis_index("head")
    piece = array.shape[split_axis] // count
    received = []
    for shift in range(count):
        target = (own + shift) % count
        part = lax.dynamic_slice_in_dim(array, target * piece, piece, split_axis)
        if shift:
            pairs = [(i, (i + shift) % count) for i in range(count)]
            part = lax.ppermute(part, "head", pairs)
        received.append(part)
    order = (own - jnp.arange(count)) % count
    stacked = jnp.take(jnp.stack(received), order, axis=0)
    stacked = jnp.moveaxis(stacked, 0, concat_axis)
    shape = list(array.shape)
    shape[split_axis] = piece
    shape[concat_axis] *= count
    return stacked.reshape(shape)


def per_chunk(queries, keys, values, output_gradient, global_blocks, random_blocks, gate):
    query_loc, key_loc, value_loc, grad_loc = (
        lax.all_to_all(queries, "head", split_axis=1, concat_axis=0, tiled=True),
        lax.all_to_all(keys, "head", split_axis=1, concat_axis=0, tiled=True),
        lax.all_to_all(values, "head", split_axis=1, concat_axis=0, tiled=True),
        lax.all_to_all(output_gradient, "head", split_axis=1, concat_axis=0, tiled=True),
    )
    if gate is not None:
        (query_loc, grad_loc), gate = lax.optimization_barrier(((query_loc, grad_loc), gate))
    shard_len, heads_q, head_width = query_loc.shape
    heads_kv = key_loc.shape[1]
    heads_per_group = heads_q // heads_kv
    kv_width = heads_kv * head_width
    blocks = shard_len // BLOCK_TOKENS
    seq_count = lax.axis_size("seq")
    own_index = lax.axis_index("seq")
    block_total_count = seq_count * blocks
    capacity = (3 * blocks + seq_count - 2) // (seq_count - 1)
    entry_count = 3 * blocks
    score_scale = 1.0 / math.sqrt(head_width)
    kv_pair = jnp.stack(
        [key_loc.reshape(shard_len, kv_width), value_loc.reshape(shard_len, kv_width)]
    )
    extended = padded(kv_pair, (("seq", 1),), BLOCK_TOKENS)
    kv_tiles = kv_pair.reshape(2, blocks, BLOCK_TOKENS, kv_width).transpose(1, 0, 2, 3)
    global_owner = global_blocks // blocks
    global_offset = global_blocks % blocks
    own_global = (jnp.arange(blocks)[None, :] == global_offset[:, None]) & (
        global_owner == own_index
    )[:, None]
    all_entries = (
        random_blocks.reshape(seq_count, blocks, 3)
        .transpose(0, 2, 1)
        .reshape(seq_count, entry_count)
    )
    all_owner = all_entries // blocks
    entry_ids = jnp.arange(entry_count)
    entry_earlier = entry_ids[None, :] < entry_ids[:, None]
    all_rank = jnp.sum(
        (all_owner[:, :, None] == all_owner[:, None, :]) & entry_earlier[None], axis=2
    )
    my_entries = lax.dynamic_index_in_dim(all_entries, own_index, 0, keepdims=False)
    my_owner = lax.dynamic_index_in_dim(all_owner, own_index, 0, keepdims=False)
    my_rank = lax.dynamic_index_in_dim(all_rank, own_index, 0, keepdims=False)
    my_slot = my_owner * capacity + my_rank
    owned_here = (all_owner == own_index)[:, :, None] & (
        all_rank[:, :, None] == jnp.arange(capacity)[None, None, :]
    )
    offset_match = (all_entries % blocks)[:, :, None] == jnp.arange(blocks)[None, None, :]
    selector = jnp.einsum(
        "tec,teo->tco",
        owned_here.astype(jnp.bfloat16),
        offset_match.astype(jnp.bfloat16),
        preferred_element_type=jnp.float32,
    ).astype(jnp.bfloat16)
    everything = lax.all_gather(kv_pair, "seq", axis=1, tiled=True)
    tiled_all = everything.reshape(2, block_total_count, BLOCK_TOKENS, kv_width)
    random_tiles = jnp.take(tiled_all, my_entries, axis=1).transpose(1, 0, 2, 3)
    global_tiles = jnp.take(tiled_all, global_blocks, axis=1).transpose(1, 0, 2, 3)
    random_by_block = random_tiles.reshape(3, blocks, 2, BLOCK_TOKENS, kv_width).transpose(
        1, 0, 2, 3, 4
    )
    block_ids = own_index * blocks + jnp.arange(blocks)
    listed = jnp.concatenate(
        [
            jnp.stack([block_ids - 1, block_ids, block_ids + 1], axis=1),
            jnp.broadcast_to(global_blocks[None, :], (blocks, 2)),
            my_entries.reshape(3, blocks).T,
        ],
        axis=1,
    )
    inside = (listed >= 0) & (listed < block_total_count)
    tile_ids = jnp.arange(8)
    tile_earlier = tile_ids[None, :] < tile_ids[:, None]
    repeat = jnp.any((listed[:, :, None] == listed[:, None, :]) & tile_earlier[None], axis=2)
    live = inside & jnp.logical_not(repeat)

    def attend(unused_state, inputs):
        query_blk, grad_blk, random_blk, live_row, position = inputs
        near_tiles = lax.dynamic_slice_in_dim(
            extended, position * BLOCK_TOKENS, 3 * BLOCK_TOKENS, 1
        )
        near_tiles = near_tiles.reshape(2, 3, BLOCK_TOKENS, kv_width).transpose(1, 0, 2, 3)
        all_tiles = jnp.concatenate([near_tiles, global_tiles, random_blk], axis=0)
        key_t = all_tiles[:, 0].reshape(8, BLOCK_TOKENS, heads_kv, head_width)
        value_t = all_tiles[:, 1].reshape(8, BLOCK_TOKENS, heads_kv, head_width)
        query_grid = query_blk.reshape(BLOCK_TOKENS, heads_kv, heads_per_group, head_width)
        grad_grid = grad_blk.reshape(BLOCK_TOKENS, heads_kv, heads_per_group, head_width)
        scores = (
            jnp.einsum("qkgd,tbkd->kgqtb", query_grid, key_t, preferred_element_type=jnp.float32)
            * score_scale
        )
        scores = jnp.where(live_row[None, None, None, :, None], scores, -jnp.inf)
        row_max = jnp.max(scores, axis=(3, 4), keepdims=True)
        expo = jnp.exp(scores - row_max)
        attn_prob = expo / jnp.sum(expo, axis=(3, 4), keepdims=True)
        prob_low = attn_prob.astype(jnp.bfloat16)
        attended = jnp.einsum(
            "kgqtb,tbkd->qkgd", prob_low, value_t, preferred_element_type=jnp.float32
        )
        out_low = attended.astype(jnp.bfloat16)
        row_delta = jnp.sum(grad_grid.astype(jnp.float32) * out_low.astype(jnp.float32), axis=-1)
        grad_prob = jnp.einsum(
            "qkgd,tbkd->kgqtb", grad_grid, value_t, preferred_element_type=jnp.float32
        )
        grad_score = attn_prob * (
            grad_prob - jnp.transpose(row_delta, (1, 2, 0))[:, :, :, None, None]
        )
        score_low = grad_score.astype(jnp.bfloat16)
        query_grad = (
            jnp.einsum("kgqtb,tbkd->qkgd", score_low, key_t, preferred_element_type=jnp.float32)
            * score_scale
        )
        key_grad = (
            jnp.einsum(
                "kgqtb,qkgd->tbkd", score_low, query_grid, preferred_element_type=jnp.float32
            )
            * score_scale
        )
        value_grad = jnp.einsum(
            "kgqtb,qkgd->tbkd", prob_low, grad_grid, preferred_element_type=jnp.float32
        )
        tile_terms = jnp.stack(
            [
                key_grad.reshape(8, BLOCK_TOKENS, kv_width),
                value_grad.reshape(8, BLOCK_TOKENS, kv_width),
            ],
            axis=1,
        )
        return (
            unused_state,
            (
                out_low.reshape(BLOCK_TOKENS, heads_q, head_width),
                query_grad.astype(jnp.bfloat16).reshape(BLOCK_TOKENS, heads_q, head_width),
                tile_terms,
            ),
        )

    unused_final, (output_block_rows, query_gradient_rows, tile_grads) = lax.scan(
        attend,
        0,
        (
            query_loc.reshape(blocks, BLOCK_TOKENS, heads_q, head_width),
            grad_loc.reshape(blocks, BLOCK_TOKENS, heads_q, head_width),
            random_by_block,
            live,
            jnp.arange(blocks),
        ),
    )
    pad_spec_low = ((0, 2), (0, 0), (0, 0), (0, 0))
    pad_spec_mid = ((1, 1), (0, 0), (0, 0), (0, 0))
    pad_spec_high = ((2, 0), (0, 0), (0, 0), (0, 0))
    window_sum = (
        jnp.pad(tile_grads[:, 0], pad_spec_low)
        + jnp.pad(tile_grads[:, 1], pad_spec_mid)
        + jnp.pad(tile_grads[:, 2], pad_spec_high)
    )
    rims = jnp.concatenate([window_sum[0], window_sum[blocks + 1]], axis=1)
    returned_rims = padded(rims.astype(jnp.bfloat16), (("seq", 1),), BLOCK_TOKENS).astype(
        rims.dtype
    )
    interior = window_sum[1 : blocks + 1]
    interior = (
        interior.at[0]
        .add(returned_rims[:, :BLOCK_TOKENS])
        .at[blocks - 1]
        .add(returned_rims[:, 3 * BLOCK_TOKENS :])
    )
    global_terms = jnp.sum(tile_grads[:, 3:5], axis=0)
    global_total = tree_sum(global_terms, "seq")
    own_weight = own_global.astype(jnp.float32)[:, :, None, None, None]
    interior = interior + jnp.sum(own_weight * global_total[:, None], axis=0)
    random_terms = (
        tile_grads[:, 5:8]
        .transpose(1, 0, 2, 3, 4)
        .reshape(entry_count, 2, BLOCK_TOKENS, kv_width)
        .astype(jnp.bfloat16)
    )
    slot_onehot = (my_slot[:, None] == jnp.arange(seq_count * capacity)[None, :]).astype(
        jnp.bfloat16
    )
    back_buffer = jnp.einsum(
        "es,exbw->sxbw", slot_onehot, random_terms, preferred_element_type=jnp.float32
    ).astype(jnp.bfloat16)
    returned_terms = lax.all_to_all(back_buffer, "seq", split_axis=0, concat_axis=0, tiled=True)
    interior = interior + jnp.einsum(
        "tco,tcxbw->oxbw",
        selector,
        returned_terms.reshape(seq_count, capacity, 2, BLOCK_TOKENS, kv_width),
        preferred_element_type=jnp.float32,
    )
    kv_grad = interior.transpose(1, 0, 2, 3).reshape(2, shard_len, kv_width).astype(jnp.bfloat16)
    out_all = output_block_rows.reshape(shard_len, heads_q, head_width)
    query_grad_all = query_gradient_rows.reshape(shard_len, heads_q, head_width)
    key_grad_all = kv_grad[0].reshape(shard_len, heads_kv, head_width)
    value_grad_all = kv_grad[1].reshape(shard_len, heads_kv, head_width)
    return ((out_all, query_grad_all, key_grad_all, value_grad_all), gate)


def head_part(array, chunks, chunk):
    tokens, heads, width = array.shape
    lanes = chunks * lax.axis_size("head")
    grid = array.reshape(tokens, lanes // chunks, chunks, heads // lanes, width)
    return grid[:, :, chunk].reshape(tokens, heads // chunks, width)


def head_join(parts):
    tokens, heads, width = parts[0].shape
    lanes = lax.axis_size("head")
    grid = jnp.stack([p.reshape(tokens, lanes, heads // lanes, width) for p in parts], axis=2)
    return grid.reshape(tokens, heads * len(parts), width)


def per_device(queries, keys, values, output_gradient, global_blocks, random_blocks):
    chunks = max(1, keys.shape[1] // lax.axis_size("head"))
    results = []
    gate = None
    for chunk in range(chunks):
        local, passed = per_chunk(
            head_part(queries, chunks, chunk),
            head_part(keys, chunks, chunk),
            head_part(values, chunks, chunk),
            head_part(output_gradient, chunks, chunk),
            global_blocks,
            random_blocks,
            gate,
        )
        if passed is not None:
            results.append(tuple((head_exchange(x, 0, 1) for x in passed)))
        gate = local
    results.append(tuple((head_exchange(x, 0, 1) for x in gate)))
    return tuple((head_join([r[i] for r in results]) for i in range(4)))


def solution(mesh):
    placed = (
        P(("seq", "head"), None, None),
        P(("seq", "head"), None, None),
        P(("seq", "head"), None, None),
        P(("seq", "head"), None, None),
        P(),
        P(),
    )
    return jax.shard_map(
        per_device,
        mesh=mesh,
        in_specs=placed,
        out_specs=(
            P(("seq", "head"), None, None),
            P(("seq", "head"), None, None),
            P(("seq", "head"), None, None),
            P(("seq", "head"), None, None),
        ),
        check_vma=False,
    )
```

profile of v0, /device:TPU:0, one launch (start us, length us, event | category | flops | bytes accessed | tf_op | source)
XLA Modules:
  0.0 592.3 jit_solution(5233339170795102321)
XLA Ops:
  9.5 6.3 %all-to-all-start.2 = ((bf16[128,4,128]{2,0,1:T(8,128)(2,1)}), bf16[128,4,128]{2,0,1:T(8,128)(2,1)S(1)}, u32[]{:S(2)}, u32[]{:S(2)}) async-start(bf16[128,4,128]{2,0,1:T(8,128)(2,1)} %bitcast.637), calls=%async_computation.2 | async-start | bytes 262144 | tf_op jit(solution)/shard_map/all_to_all | solution.py:65
  17.4 4.5 all-to-all-done.2
  21.9 8.4 %all_to_all.136 = bf16[128,4,128]{2,0,1:T(8,128)(2,1)S(1)} all-to-all(bf16[128,4,128]{2,0,1:T(8,128)(2,1)S(1)} %bitcast.819), channel_id=1, replica_groups=mesh['seq'=8,'head'=4] {'head'}, dimensions={1} | all-to-all | bytes 262144 | tf_op jit(solution)/shard_map/all_to_all | solution.py:66
  35.8 5.2 all-to-all-done.7
  46.7 4.2 all-to-all-done.8
  50.9 4.2 all-to-all-start.4
  56.9 20.2 %all-to-all-done.4 = bf16[128,32,128]{2,0,1:T(8,128)(2,1)} async-done(((bf16[128,32,128]{2,0,1:T(8,128)(2,1)}), bf16[128,32,128]{2,0,1:T(8,128)(2,1)}, u32[]{:S(2)}, u32[]{:S(2)}) %all-to-all-start.4) | async-done | bytes 1048608 | tf_op jit(solution)/shard_map/all_to_all | solution.py:64
  90.6 13.8 %all-to-all-done = bf16[128,32,128]{2,0,1:T(8,128)(2,1)S(1)} async-done(((bf16[128,32,128]{2,0,1:T(8,128)(2,1)}), bf16[128,32,128]{2,0,1:T(8,128)(2,1)S(1)}, u32[]{:S(2)}, u32[]{:S(2)}) %all-to-all-start) | async-done | bytes 1048608 | tf_op jit(solution)/shard_map/all_to_all | solution.py:64
  116.1 17.1 %all-to-all-done.1 = bf16[128,32,128]{2,0,1:T(8,128)(2,1)S(1)} async-done(((bf16[128,32,128]{2,0,1:T(8,128)(2,1)}), bf16[128,32,128]{2,0,1:T(8,128)(2,1)S(1)}, u32[]{:S(2)}, u32[]{:S(2)}) %all-to-all-start.1) | async-done | bytes 1048608 | tf_op jit(solution)/shard_map/all_to_all | solution.py:67
  133.2 4.3 all-to-all-start.5
  142.0 4.6 collective-permute-start.10
  172.1 89.8 %while.32 = (s32[]{:T(128)}, bf16[4,128,8,128]{3,2,1,0:T(8,128)(2,1)}, bf16[4,128,8,128]{3,2,1,0:T(8,128)(2,1)}, f32[4,8,2,128,128]{3,4,1,2,0:T(8,128)}, s32[4]{...) while((s32[]{:T(128)}, ...), condition=%wide.region_5.8_spmd, body=%wide.region_1.7_spmd.sunk | while | flops 1632367616 | bytes 61382416 | solution.py:200
  263.1 5.4 copy.496
  278.2 6.1 %collective-permute-start.5 = (bf16[2,2,128,128]{2,3,0,1:T(8,128)(2,1)S(1)}, bf16[2,2,128,128]{2,3,0,1:T(8,128)(2,1)S(1)}, u32[]{:S(2)}, u32[]{:S(2)}) collective-permute-start(bf16[2,2,128,128]{2,3,0,1:T(8,128)(2,1)S(1)} %fusion.89), channel_id=1, source_target_pairs={{0,8},{4,12},{8,0},{12,4},{16,24},{20,28},{24,16},{28,20},{1,9},{5... | collective-permute-start | bytes 393224 | tf_op jit(solution)/shard_map/ppermute | solution.py:35
  295.7 11.4 %collective-permute-done.6 = bf16[2,2,128,128]{2,3,0,1:T(8,128)(2,1)S(1)} collective-permute-done((bf16[2,2,128,128]{2,3,0,1:T(8,128)(2,1)S(1)}, bf16[2,2,128,128]{2,3,0,1:T(8,128)(2,1)S(1)}, u32[]{:S(2)}, u32[]{:S(2)}) %collective-permute-start.6) | collective-permute-done | bytes 131104 | tf_op jit(solution)/shard_map/ppermute | solution.py:35
  314.7 109.1 %while.33 = (s32[]{:T(128)}, bf16[4,128,8,128]{3,2,1,0:T(8,128)(2,1)}, bf16[4,128,8,128]{3,2,1,0:T(8,128)(2,1)}, f32[4,8,2,128,128]{3,4,1,2,0:T(8,128)}, s32[4]{...) while((s32[]{:T(128)}, ...), condition=%wide.region_13.17_spmd, body=%wide.region_9.16_spmd.sunk | while | flops 1632367616 | bytes 79207432 | solution.py:200
  425.2 5.4 copy.529
  447.2 4.2 all-to-all-start.9
  478.4 6.5 %collective-permute-done.8 = bf16[128,8,128]{2,1,0:T(8,128)(2,1)} collective-permute-done((bf16[128,8,128]{2,1,0:T(8,128)(2,1)S(1)}, bf16[128,8,128]{2,1,0:T(8,128)(2,1)}, u32[]{:S(2)}, u32[]{:S(2)}) %collective-permute-start.8) | collective-permute-done | bytes 262176 | tf_op jit(solution)/shard_map/ppermute | solution.py:51
  488.9 14.7 %collective-permute-start.13 = (bf16[128,8,128]{2,1,0:T(8,128)(2,1)}, bf16[128,8,128]{2,1,0:T(8,128)(2,1)}, u32[]{:S(2)}, u32[]{:S(2)}) collective-permute-start(bf16[128,8,128]{2,1,0:T(8,128)(2,1)} %get-tuple-element.456), channel_id=1, source_target_pairs={{0,2},{1,3},{2,0},{3,1},{4,6},{5,7},{6,4},{7,5},{8,10},{9,11},{10,... | collective-permute-start | bytes 786440 | tf_op jit(solution)/shard_map/ppermute | solution.py:51
  506.1 12.5 %collective-permute-done.19 = bf16[128,8,128]{2,1,0:T(8,128)(2,1)S(1)} collective-permute-done((bf16[128,8,128]{2,1,0:T(8,128)(2,1)}, bf16[128,8,128]{2,1,0:T(8,128)(2,1)S(1)}, u32[]{:S(2)}, u32[]{:S(2)}) %collective-permute-start.19) | collective-permute-done | bytes 262176 | tf_op jit(solution)/shard_map/ppermute | solution.py:51
  534.5 6.7 %collective-permute-done.13 = bf16[128,8,128]{2,1,0:T(8,128)(2,1)} collective-permute-done((bf16[128,8,128]{2,1,0:T(8,128)(2,1)}, bf16[128,8,128]{2,1,0:T(8,128)(2,1)}, u32[]{:S(2)}, u32[]{:S(2)}) %collective-permute-start.13) | collective-permute-done | bytes 262176 | tf_op jit(solution)/shard_map/ppermute | solution.py:51
  548.0 4.4 collective-permute-done.16
  567.2 6.1 %collective-permute-start.35 = (bf16[128,1,128]{2,0,1:T(8,128)(2,1)S(1)}, bf16[128,1,128]{2,0,1:T(8,128)(2,1)S(1)}, u32[]{:S(2)}, u32[]{:S(2)}) collective-permute-start(bf16[128,1,128]{2,0,1:T(8,128)(2,1)S(1)} %get-tuple-element.481), channel_id=1, source_target_pairs={{0,1},{1,2},{2,3},{3,0},{4,5},{5,6},{6,7},{7,4},{8,9},{9,10},{10,1... | collective-permute-start | bytes 98312 | tf_op jit(solution)/shard_map/ppermute | solution.py:51
  (506 shorter events, 394.4 us)
Async XLA Ops:
  15.8 140.3 %all-gather.3.cloned.1.call-start = ((), (), s32[]{:S(2)}) async-start(), calls=%async_computation.10 | async-start | bytes 2359296 | tf_op jit(solution)/shard_map/all_gather | solution.py:117
  50.9 26.2 %all-to-all-start.4 = ((bf16[128,32,128]{2,0,1:T(8,128)(2,1)}), bf16[128,32,128]{2,0,1:T(8,128)(2,1)}, u32[]{:S(2)}, u32[]{:S(2)}) async-start(bf16[128,32,128]{2,0,1:T(8,128)(2,1)} %bitcast.135), calls=%async_computation.4 | async-start | bytes 2097152 | tf_op jit(solution)/shard_map/all_to_all | solution.py:64
  77.1 27.3 %all-to-all-start = ((bf16[128,32,128]{2,0,1:T(8,128)(2,1)}), bf16[128,32,128]{2,0,1:T(8,128)(2,1)S(1)}, u32[]{:S(2)}, u32[]{:S(2)}) async-start(bf16[128,32,128]{2,0,1:T(8,128)(2,1)} %bitcast.105), calls=%async_computation | async-start | bytes 2097152 | tf_op jit(solution)/shard_map/all_to_all | solution.py:64
  80.6 77.8 %all-gather.5.cloned.1.call-start = ((), (), s32[]{:S(2)}) async-start(), calls=%async_computation.11 | async-start | bytes 2359296 | tf_op jit(solution)/shard_map/all_gather | solution.py:117
  104.4 28.8 %all-to-all-start.1 = ((bf16[128,32,128]{2,0,1:T(8,128)(2,1)}), bf16[128,32,128]{2,0,1:T(8,128)(2,1)S(1)}, u32[]{:S(2)}, u32[]{:S(2)}) async-start(bf16[128,32,128]{2,0,1:T(8,128)(2,1)} %bitcast.111), calls=%async_computation.1 | async-start | bytes 2097152 | tf_op jit(solution)/shard_map/all_to_all | solution.py:67
  133.2 34.1 %all-to-all-start.5 = ((bf16[128,32,128]{0,2,1:T(8,128)(2,1)}), bf16[128,32,128]{0,2,1:T(8,128)(2,1)}, u32[]{:S(2)}, u32[]{:S(2)}) async-start(bf16[128,32,128]{0,2,1:T(8,128)(2,1)} %bitcast.138), calls=%async_computation.5 | async-start | bytes 2097152 | tf_op jit(solution)/shard_map/all_to_all | solution.py:67
  286.2 21.3 %all-to-all-start.6 = ((bf16[16,2,128,128]{3,2,1,0:T(8,128)(2,1)}), bf16[16,2,128,128]{3,2,1,0:T(8,128)(2,1)S(1)}, u32[]{:S(2)}, u32[]{:S(2)}) async-start(bf16[16,2,128,128]{3,2,1,0:T(8,128)(2,1)} %copy.513), calls=%async_computation.6 | async-start | bytes 2097152 | tf_op jit(solution)/shard_map/all_to_all | solution.py:246
  434.3 21.3 %collective-permute-start.21 = (bf16[128,1,128]{2,0,1:T(8,128)(2,1)}, bf16[128,1,128]{2,0,1:T(8,128)(2,1)}, u32[]{:S(2)}, u32[]{:S(2)}) collective-permute-start(bf16[128,1,128]{2,0,1:T(8,128)(2,1)} %get-tuple-element.485), channel_id=1, source_target_pairs={{0,1},{1,2},{2,3},{3,0},{4,5},{5,6},{6,7},{7,4},{8,9},{9,10},{10,1... | collective-permute-start | bytes 98312 | tf_op jit(solution)/shard_map/ppermute | solution.py:51
  436.3 19.9 %collective-permute-start.22 = (bf16[128,1,128]{2,0,1:T(8,128)(2,1)}, bf16[128,1,128]{2,0,1:T(8,128)(2,1)}, u32[]{:S(2)}, u32[]{:S(2)}) collective-permute-start(bf16[128,1,128]{2,0,1:T(8,128)(2,1)} %get-tuple-element.484), channel_id=1, source_target_pairs={{0,2},{1,3},{2,0},{3,1},{4,6},{5,7},{6,4},{7,5},{8,10},{9,11},{10,... | collective-permute-start | bytes 98312 | tf_op jit(solution)/shard_map/ppermute | solution.py:51
  440.4 33.2 %collective-permute-start.26 = (bf16[2,2,128,128]{2,3,0,1:T(8,128)(2,1)}, bf16[2,2,128,128]{2,3,0,1:T(8,128)(2,1)S(1)}, u32[]{:S(2)}, u32[]{:S(2)}) collective-permute-start(bf16[2,2,128,128]{2,3,0,1:T(8,128)(2,1)} %convert_element_type.207), channel_id=1, source_target_pairs={{0,4},{4,0},{8,12},{12,8},{16,20},{20,16},{24,28},{28,24},{1,5},{5... | collective-permute-start | bytes 393224 | tf_op jit(solution)/shard_map/ppermute | solution.py:35
  442.1 24.4 %collective-permute-start.24 = (bf16[2,128,128]{2,1,0:T(8,128)(2,1)}, bf16[2,128,128]{2,1,0:T(8,128)(2,1)}, u32[]{:S(2)}, u32[]{:S(2)}) collective-permute-start(bf16[2,128,128]{2,1,0:T(8,128)(2,1)} %get-tuple-element.458), channel_id=1, source_target_pairs={{0,4},{4,8},{8,12},{12,16},{16,20},{20,24},{24,28},{1,5},{5,9},{9,... | collective-permute-start | bytes 196616 | tf_op jit(solution)/shard_map/ppermute | solution.py:17
  447.2 117.6 %all-to-all-start.9 = ((bf16[16,2,128,128]{3,2,1,0:T(8,128)(2,1)}), bf16[16,2,128,128]{3,2,1,0:T(8,128)(2,1)}, u32[]{:S(2)}, u32[]{:S(2)}) async-start(bf16[16,2,128,128]{3,2,1,0:T(8,128)(2,1)} %copy.538), calls=%async_computation.9 | async-start | bytes 2097152 | tf_op jit(solution)/shard_map/all_to_all | solution.py:246
  463.5 21.5 %collective-permute-start.8 = (bf16[128,8,128]{2,1,0:T(8,128)(2,1)S(1)}, bf16[128,8,128]{2,1,0:T(8,128)(2,1)}, u32[]{:S(2)}, u32[]{:S(2)}) collective-permute-start(bf16[128,8,128]{2,1,0:T(8,128)(2,1)S(1)} %copy-done.21), channel_id=1, source_target_pairs={{0,2},{1,3},{2,0},{3,1},{4,6},{5,7},{6,4},{7,5},{8,10},{9,11},{10,... | collective-permute-start | bytes 786440 | tf_op jit(solution)/shard_map/ppermute | solution.py:51
  466.5 22.4 %collective-permute-start.9 = (bf16[128,8,128]{2,1,0:T(8,128)(2,1)S(1)}, bf16[128,8,128]{2,1,0:T(8,128)(2,1)}, u32[]{:S(2)}, u32[]{:S(2)}) collective-permute-start(bf16[128,8,128]{2,1,0:T(8,128)(2,1)S(1)} %copy-done.20), channel_id=1, source_target_pairs={{0,3},{1,0},{2,1},{3,2},{4,7},{5,4},{6,5},{7,6},{8,11},{9,8},{10,9... | collective-permute-start | bytes 786440 | tf_op jit(solution)/shard_map/ppermute | solution.py:51
  469.1 35.7 %collective-permute-start.18 = (bf16[128,8,128]{2,1,0:T(8,128)(2,1)}, bf16[128,8,128]{2,1,0:T(8,128)(2,1)}, u32[]{:S(2)}, u32[]{:S(2)}) collective-permute-start(bf16[128,8,128]{2,1,0:T(8,128)(2,1)} %get-tuple-element.449), channel_id=1, source_target_pairs={{0,1},{1,2},{2,3},{3,0},{4,5},{5,6},{6,7},{7,4},{8,9},{9,10},{10,1... | collective-permute-start | bytes 786440 | tf_op jit(solution)/shard_map/ppermute | solution.py:51
  473.7 44.9 %collective-permute-start.19 = (bf16[128,8,128]{2,1,0:T(8,128)(2,1)}, bf16[128,8,128]{2,1,0:T(8,128)(2,1)S(1)}, u32[]{:S(2)}, u32[]{:S(2)}) collective-permute-start(bf16[128,8,128]{2,1,0:T(8,128)(2,1)} %get-tuple-element.448), channel_id=1, source_target_pairs={{0,2},{1,3},{2,0},{3,1},{4,6},{5,7},{6,4},{7,5},{8,10},{9,11},{10,... | collective-permute-start | bytes 786440 | tf_op jit(solution)/shard_map/ppermute | solution.py:51
  474.8 47.9 %collective-permute-start.20 = (bf16[128,8,128]{2,1,0:T(8,128)(2,1)S(1)}, bf16[128,8,128]{2,1,0:T(8,128)(2,1)S(1)}, u32[]{:S(2)}, u32[]{:S(2)}) collective-permute-start(bf16[128,8,128]{2,1,0:T(8,128)(2,1)S(1)} %get-tuple-element.447), channel_id=1, source_target_pairs={{0,3},{1,0},{2,1},{3,2},{4,7},{5,4},{6,5},{7,6},{8,11},{9,8},{10,9... | collective-permute-start | bytes 786440 | tf_op jit(solution)/shard_map/ppermute | solution.py:51
  485.0 47.0 %collective-permute-start.12 = (bf16[128,8,128]{2,1,0:T(8,128)(2,1)}, bf16[128,8,128]{2,1,0:T(8,128)(2,1)}, u32[]{:S(2)}, u32[]{:S(2)}) collective-permute-start(bf16[128,8,128]{2,1,0:T(8,128)(2,1)} %get-tuple-element.457), channel_id=1, source_target_pairs={{0,1},{1,2},{2,3},{3,0},{4,5},{5,6},{6,7},{7,4},{8,9},{9,10},{10,1... | collective-permute-start | bytes 786440 | tf_op jit(solution)/shard_map/ppermute | solution.py:51
  488.9 52.3 %collective-permute-start.13 = (bf16[128,8,128]{2,1,0:T(8,128)(2,1)}, bf16[128,8,128]{2,1,0:T(8,128)(2,1)}, u32[]{:S(2)}, u32[]{:S(2)}) collective-permute-start(bf16[128,8,128]{2,1,0:T(8,128)(2,1)} %get-tuple-element.456), channel_id=1, source_target_pairs={{0,2},{1,3},{2,0},{3,1},{4,6},{5,7},{6,4},{7,5},{8,10},{9,11},{10,... | collective-permute-start | bytes 786440 | tf_op jit(solution)/shard_map/ppermute | solution.py:51
  504.9 38.8 %collective-permute-start.14 = (bf16[128,8,128]{2,1,0:T(8,128)(2,1)}, bf16[128,8,128]{2,1,0:T(8,128)(2,1)}, u32[]{:S(2)}, u32[]{:S(2)}) collective-permute-start(bf16[128,8,128]{2,1,0:T(8,128)(2,1)} %get-tuple-element.455), channel_id=1, source_target_pairs={{0,3},{1,0},{2,1},{3,2},{4,7},{5,4},{6,5},{7,6},{8,11},{9,8},{10,9... | collective-permute-start | bytes 786440 | tf_op jit(solution)/shard_map/ppermute | solution.py:51
  518.6 29.4 %collective-permute-start.15 = (bf16[128,8,128]{2,1,0:T(8,128)(2,1)}, bf16[128,8,128]{2,1,0:T(8,128)(2,1)}, u32[]{:S(2)}, u32[]{:S(2)}) collective-permute-start(bf16[128,8,128]{2,1,0:T(8,128)(2,1)} %get-tuple-element.445), channel_id=1, source_target_pairs={{0,1},{1,2},{2,3},{3,0},{4,5},{5,6},{6,7},{7,4},{8,9},{9,10},{10,1... | collective-permute-start | bytes 786440 | tf_op jit(solution)/shard_map/ppermute | solution.py:51
  528.7 23.7 %collective-permute-start.16 = (bf16[128,8,128]{2,1,0:T(8,128)(2,1)}, bf16[128,8,128]{2,1,0:T(8,128)(2,1)}, u32[]{:S(2)}, u32[]{:S(2)}) collective-permute-start(bf16[128,8,128]{2,1,0:T(8,128)(2,1)} %get-tuple-element.444), channel_id=1, source_target_pairs={{0,2},{1,3},{2,0},{3,1},{4,6},{5,7},{6,4},{7,5},{8,10},{9,11},{10,... | collective-permute-start | bytes 786440 | tf_op jit(solution)/shard_map/ppermute | solution.py:51
  531.9 20.4 %collective-permute-start.17 = (bf16[128,8,128]{2,1,0:T(8,128)(2,1)}, bf16[128,8,128]{2,1,0:T(8,128)(2,1)}, u32[]{:S(2)}, u32[]{:S(2)}) collective-permute-start(bf16[128,8,128]{2,1,0:T(8,128)(2,1)} %get-tuple-element.443), channel_id=1, source_target_pairs={{0,3},{1,0},{2,1},{3,2},{4,7},{5,4},{6,5},{7,6},{8,11},{9,8},{10,9... | collective-permute-start | bytes 786440 | tf_op jit(solution)/shard_map/ppermute | solution.py:51
  541.2 22.3 %collective-permute-start.28 = (bf16[2,2,128,128]{2,3,0,1:T(8,128)(2,1)}, bf16[2,2,128,128]{2,3,0,1:T(8,128)(2,1)}, u32[]{:S(2)}, u32[]{:S(2)}) collective-permute-start(bf16[2,2,128,128]{2,3,0,1:T(8,128)(2,1)} %fusion.100), channel_id=1, source_target_pairs={{0,16},{4,20},{8,24},{12,28},{16,0},{20,4},{24,8},{28,12},{1,17},{... | collective-permute-start | bytes 393224 | tf_op jit(solution)/shard_map/ppermute | solution.py:35
  (78 other events, 958.8 us)
Sparse Core Ops, SparseCore 0:
  31.2 26.8 all-gather.2
  84.2 29.0 all-gather.4
where the time goes:
time: 601 us; the launch traced here: 592 us
  local copies, waits for them, and re-layouts  168 us (28%)
  starting transfers between devices  129 us (21%)
  waiting for transfers between devices  112 us (19%)
  matrix products  86.2 us (14%)
  other arithmetic  67.2 us (11%)
  between operations  15.3 us (3%)
  blocking collectives  8.43 us (1%)
  loops' own time  6.06 us (1%)
    ppermute x24, starting transfers between devices, head_exchange(): part = lax.ppermute(part, 'head', pairs)  58.8 us
    another operation x20, local copies, waits for them, and re-layouts  35.9 us
    all_to_all x2, waiting for transfers between devices, per_chunk(): lax.all_to_all(queries, 'head', split_axis=1, concat_axis=0, tiled=True)  34 us
    ppermute x24, waiting for transfers between devices, head_exchange(): part = lax.ppermute(part, 'head', pairs)  32.7 us
    dot_general x8, matrix products, attend(): jnp.einsum('qkgd,tbkd->kgqtb', grad_grid, value_t, preferred_element_type...  28.5 us
    dot_general x8, matrix products, attend(): jnp.einsum('kgqtb,qkgd->tbkd', prob_low, grad_grid, preferred_element_typ...  17.2 us
    all_to_all x2, waiting for transfers between devices, per_chunk(): lax.all_to_all(output_gradient, 'head', split_axis=1, concat_axis=0, tile...  17.1 us
    dynamic_slice x24, local copies, waits for them, and re-layouts, per_chunk(): lax.scan(attend, 0, (query_loc.reshape(blocks, BLOCK_TOKENS, heads_q, hea...  16.8 us
  transfers between devices with their start and end apart: 49, of which 16 were waited for; matrix products, arithmetic and copies ran while one was open for 15% of the time, Pallas kernels for 0%

commit v1 on v0

--- a/solution.py
+++ b/solution.py
@@ -61,7 +61,12 @@
 
 def per_chunk(queries, keys, values, output_gradient, global_blocks, random_blocks, gate):
     query_loc, key_loc, value_loc, grad_loc = (
-        lax.all_to_all(queries, "head", split_axis=1, concat_axis=0, tiled=True),
+        jnp.concatenate(
+            lax.all_to_all(
+                jnp.stack(jnp.split(queries, lax.axis_size("head"), axis=1)), "head", 0, 0
+            ),
+            axis=0,
+        ),
         lax.all_to_all(keys, "head", split_axis=1, concat_axis=0, tiled=True),
         lax.all_to_all(values, "head", split_axis=1, concat_axis=0, tiled=True),
         lax.all_to_all(output_gradient, "head", split_axis=1, concat_axis=0, tiled=True),

time: 601 us -> 552 us (0.918)
  waiting for transfers between devices: 112 us -> 54.7 us
  starting transfers between devices: 129 us -> 136 us
    all_to_all x2, waiting for transfers between devices: 34 us -> 13 us  [per_chunk(): lax.all_to_all(jnp.stack(jnp.split(queries, lax.axis_size('head'), axis=1...]
    all_to_all x2, waiting for transfers between devices: 17.1 us -> 0.46 us  [per_chunk(): lax.all_to_all(output_gradient, 'head', split_axis=1, concat_axis=0, tile...]
    ppermute x6, waiting for transfers between devices: 12 us -> 0.59 us  [tree_sum(): other = lax.ppermute(part.astype(jnp.bfloat16), axis, pairs)]
    ppermute x24, waiting for transfers between devices: 32.7 us -> 26 us  [head_exchange(): part = lax.ppermute(part, 'head', pairs)]
    another operation x20 -> x22, local copies, waits for them, and re-layouts: 35.9 us -> 36.1 us
  transfers between devices with their start and end apart: 49 -> 49, of which waited for: 16 -> 14; matrix products, arithmetic and copies ran while one was open for 15% -> 35% of each run, Pallas kernels for 0% -> 0%
where the time goes in v1:
time: 552 us; the launch traced here: 541 us
  local copies, waits for them, and re-layouts  163 us (30%)
  starting transfers between devices  136 us (25%)
  matrix products  85.5 us (15%)
  other arithmetic  72.8 us (13%)
  waiting for transfers between devices  54.7 us (10%)
  between operations  15.3 us (3%)
  blocking collectives  8.43 us (2%)
  loops' own time  6.28 us (1%)
    ppermute x24, starting transfers between devices, head_exchange(): part = lax.ppermute(part, 'head', pairs)  58.2 us
    another operation x20, local copies, waits for them, and re-layouts  35.8 us
    dot_general x8, matrix products, attend(): jnp.einsum('qkgd,tbkd->kgqtb', grad_grid, value_t, preferred_element_type...  28.4 us
    ppermute x24, waiting for transfers between devices, head_exchange(): part = lax.ppermute(part, 'head', pairs)  26 us
    dot_general x8, matrix products, attend(): jnp.einsum('kgqtb,qkgd->tbkd', prob_low, grad_grid, preferred_element_typ...  17.2 us
    ppermute x6, starting transfers between devices, tree_sum(): other = lax.ppermute(part.astype(jnp.bfloat16), axis, pairs)  17.2 us
    dynamic_slice x24, local copies, waits for them, and re-layouts, per_chunk(): lax.scan(attend, 0, (query_loc.reshape(blocks, BLOCK_TOKENS, heads_q, hea...  16.8 us
    dot_general x8, matrix products, attend(): jnp.einsum('kgqtb,qkgd->tbkd', score_low, query_grid, preferred_element_t...  13.6 us
  transfers between devices with their start and end apart: 49, of which 14 were waited for; matrix products, arithmetic and copies ran while one was open for 35% of the time, Pallas kernels for 0%

profile of v1, /device:TPU:0, one launch (start us, length us, event | category | flops | bytes accessed | tf_op | source)
XLA Modules:
  0.0 541.3 jit_solution(15844338955871956948)
XLA Ops:
  9.4 6.3 %all-to-all-start.2 = ((bf16[128,4,128]{2,0,1:T(8,128)(2,1)}), bf16[128,4,128]{2,0,1:T(8,128)(2,1)S(1)}, u32[]{:S(2)}, u32[]{:S(2)}) async-start(bf16[128,4,128]{2,0,1:T(8,128)(2,1)} %bitcast.648), calls=%async_computation.2 | async-start | bytes 262144 | tf_op jit(solution)/shard_map/all_to_all | solution.py:70
  17.3 4.5 all-to-all-done.2
  21.8 8.4 %all_to_all.113 = bf16[128,4,128]{2,0,1:T(8,128)(2,1)S(1)} all-to-all(bf16[128,4,128]{2,0,1:T(8,128)(2,1)S(1)} %bitcast.833), channel_id=1, replica_groups=mesh['seq'=8,'head'=4] {'head'}, dimensions={1} | all-to-all | bytes 262144 | tf_op jit(solution)/shard_map/all_to_all | solution.py:71
  41.5 4.9 all-to-all-start.8
  52.3 4.3 all-to-all-start.4
  73.7 5.2 all-to-all-done.4
  78.9 4.3 all-to-all-start.5
  89.2 5.4 collective-permute-start.10
  107.5 5.1 all-to-all-start.1
  117.4 87.5 %while.32 = (s32[]{:T(128)}, bf16[4,128,8,128]{3,2,1,0:T(8,128)(2,1)}, bf16[4,128,8,128]{3,2,1,0:T(8,128)(2,1)}, f32[4,8,2,128,128]{3,4,1,2,0:T(8,128)}, s32[4]{...) while((s32[]{:T(128)}, ...), condition=%wide.region_5.8_spmd, body=%wide.region_1.7_spmd.sunk | while | flops 1632367616 | bytes 61382912 | solution.py:205
  204.9 5.4 copy.482
  213.8 6.5 %all-to-all-start.6 = ((bf16[16,2,128,128]{3,2,1,0:T(8,128)(2,1)}), bf16[16,2,128,128]{3,2,1,0:T(8,128)(2,1)S(1)}, u32[]{:S(2)}, u32[]{:S(2)}) async-start(bf16[16,2,128,128]{3,2,1,0:T(8,128)(2,1)} %copy.499), calls=%async_computation.6 | async-start | bytes 2097152 | tf_op jit(solution)/shard_map/all_to_all | solution.py:251
  230.6 5.5 %all-to-all-done.6 = bf16[16,2,128,128]{3,2,1,0:T(8,128)(2,1)S(1)} async-done(((bf16[16,2,128,128]{3,2,1,0:T(8,128)(2,1)}), bf16[16,2,128,128]{3,2,1,0:T(8,128)(2,1)S(1)}, u32[]{:S(2)}, u32[]{:S(2)}) %all-to-all-start.6) | async-done | bytes 1048608 | tf_op jit(solution)/shard_map/all_to_all | solution.py:251
  236.2 5.1 all-to-all-start
  245.1 4.5 collective-permute-start.6
  256.0 7.8 %all-to-all-done = bf16[4,128,8,128]{3,2,1,0:T(8,128)(2,1)} async-done(((bf16[4,128,8,128]{3,2,1,0:T(8,128)(2,1)}), bf16[4,128,8,128]{3,2,1,0:T(8,128)(2,1)}, u32[]{:S(2)}, u32[]{:S(2)}) %all-to-all-start) | async-done | bytes 1048608 | tf_op jit(solution)/shard_map/all_to_all | solution.py:65
  268.5 106.5 %while.33 = (s32[]{:T(128)}, bf16[4,128,8,128]{3,2,1,0:T(8,128)(2,1)}, bf16[4,128,8,128]{3,2,1,0:T(8,128)(2,1)}, f32[4,8,2,128,128]{3,4,1,2,0:T(8,128)}, s32[4]{...) while((s32[]{:T(128)}, ...), condition=%wide.region_13.17_spmd, body=%wide.region_9.16_spmd.sunk | while | flops 1632367616 | bytes 79207600 | solution.py:205
  376.4 5.4 copy.515
  428.9 5.4 %collective-permute-done.8 = bf16[128,8,128]{2,1,0:T(8,128)(2,1)} collective-permute-done((bf16[128,8,128]{2,1,0:T(8,128)(2,1)S(1)}, bf16[128,8,128]{2,1,0:T(8,128)(2,1)}, u32[]{:S(2)}, u32[]{:S(2)}) %collective-permute-start.8) | collective-permute-done | bytes 262176 | tf_op jit(solution)/shard_map/ppermute | solution.py:51
  437.3 13.3 %collective-permute-start.13 = (bf16[128,8,128]{2,1,0:T(8,128)(2,1)}, bf16[128,8,128]{2,1,0:T(8,128)(2,1)}, u32[]{:S(2)}, u32[]{:S(2)}) collective-permute-start(bf16[128,8,128]{2,1,0:T(8,128)(2,1)} %get-tuple-element.456), channel_id=1, source_target_pairs={{0,2},{1,3},{2,0},{3,1},{4,6},{5,7},{6,4},{7,5},{8,10},{9,11},{10,... | collective-permute-start | bytes 786440 | tf_op jit(solution)/shard_map/ppermute | solution.py:51
  455.3 12.5 %collective-permute-done.19 = bf16[128,8,128]{2,1,0:T(8,128)(2,1)S(1)} collective-permute-done((bf16[128,8,128]{2,1,0:T(8,128)(2,1)}, bf16[128,8,128]{2,1,0:T(8,128)(2,1)S(1)}, u32[]{:S(2)}, u32[]{:S(2)}) %collective-permute-start.19) | collective-permute-done | bytes 262176 | tf_op jit(solution)/shard_map/ppermute | solution.py:51
  471.1 5.1 collective-permute-start.27
  489.0 5.3 collective-permute-start.28
  516.5 6.2 %collective-permute-start.35 = (bf16[128,1,128]{2,0,1:T(8,128)(2,1)S(1)}, bf16[128,1,128]{2,0,1:T(8,128)(2,1)S(1)}, u32[]{:S(2)}, u32[]{:S(2)}) collective-permute-start(bf16[128,1,128]{2,0,1:T(8,128)(2,1)S(1)} %get-tuple-element.489), channel_id=1, source_target_pairs={{0,1},{1,2},{2,3},{3,0},{4,5},{5,6},{6,7},{7,4},{8,9},{9,10},{10,1... | collective-permute-start | bytes 98312 | tf_op jit(solution)/shard_map/ppermute | solution.py:51
  (560 shorter events, 383.3 us)
Async XLA Ops:
  15.7 80.2 %all-gather.3.cloned.1.call-start = ((), (), s32[]{:S(2)}) async-start(), calls=%async_computation.10 | async-start | bytes 2359296 | tf_op jit(solution)/shard_map/all_gather | solution.py:122
  52.3 26.6 %all-to-all-start.4 = ((bf16[4,128,8,128]{3,1,2,0:T(8,128)(2,1)}), bf16[4,128,8,128]{3,1,2,0:T(8,128)(2,1)}, u32[]{:S(2)}, u32[]{:S(2)}) async-start(bf16[4,128,8,128]{3,1,2,0:T(8,128)(2,1)} %pad_maximum_fusion.5), calls=%async_computation.4 | async-start | bytes 2097152 | tf_op jit(solution)/shard_map/all_to_all | solution.py:65
  56.6 41.7 %all-gather.5.cloned.1.call-start = ((), (), s32[]{:S(2)}) async-start(), calls=%async_computation.11 | async-start | bytes 2359296 | tf_op jit(solution)/shard_map/all_gather | solution.py:122
  78.9 28.5 %all-to-all-start.5 = ((bf16[128,32,128]{0,2,1:T(8,128)(2,1)}), bf16[128,32,128]{0,2,1:T(8,128)(2,1)}, u32[]{:S(2)}, u32[]{:S(2)}) async-start(bf16[128,32,128]{0,2,1:T(8,128)(2,1)} %bitcast.141), calls=%async_computation.5 | async-start | bytes 2097152 | tf_op jit(solution)/shard_map/all_to_all | solution.py:72
  89.2 131.0 %collective-permute-start.10 = (bf16[2,128,128]{2,1,0:T(8,128)(2,1)}, bf16[2,128,128]{2,1,0:T(8,128)(2,1)}, u32[]{:S(2)}, u32[]{:S(2)}) collective-permute-start(bf16[2,128,128]{2,1,0:T(8,128)(2,1)} %get-tuple-element.480), channel_id=1, source_target_pairs={{0,4},{4,8},{8,12},{12,16},{16,20},{20,24},{24,28},{1,5},{5,9},{9,... | collective-permute-start | bytes 196616 | tf_op jit(solution)/shard_map/ppermute | solution.py:17
  94.6 125.7 %collective-permute-start.11 = (bf16[2,128,128]{2,1,0:T(8,128)(2,1)}, bf16[2,128,128]{2,1,0:T(8,128)(2,1)}, u32[]{:S(2)}, u32[]{:S(2)}) collective-permute-start(bf16[2,128,128]{2,1,0:T(8,128)(2,1)} %get-tuple-element.481), channel_id=1, source_target_pairs={{4,0},{8,4},{12,8},{16,12},{20,16},{24,20},{28,24},{5,1},{9,5},{13... | collective-permute-start | bytes 196616 | tf_op jit(solution)/shard_map/ppermute | solution.py:18
  107.5 106.3 %all-to-all-start.1 = ((bf16[128,32,128]{2,0,1:T(8,128)(2,1)}), bf16[128,32,128]{2,0,1:T(8,128)(2,1)}, u32[]{:S(2)}, u32[]{:S(2)}) async-start(bf16[128,32,128]{2,0,1:T(8,128)(2,1)} %bitcast.112), calls=%async_computation.1 | async-start | bytes 2097152 | tf_op jit(solution)/shard_map/all_to_all | solution.py:72
  213.8 22.4 %all-to-all-start.6 = ((bf16[16,2,128,128]{3,2,1,0:T(8,128)(2,1)}), bf16[16,2,128,128]{3,2,1,0:T(8,128)(2,1)S(1)}, u32[]{:S(2)}, u32[]{:S(2)}) async-start(bf16[16,2,128,128]{3,2,1,0:T(8,128)(2,1)} %copy.499), calls=%async_computation.6 | async-start | bytes 2097152 | tf_op jit(solution)/shard_map/all_to_all | solution.py:251
  236.2 27.6 %all-to-all-start = ((bf16[4,128,8,128]{3,2,1,0:T(8,128)(2,1)}), bf16[4,128,8,128]{3,2,1,0:T(8,128)(2,1)}, u32[]{:S(2)}, u32[]{:S(2)}) async-start(bf16[4,128,8,128]{3,2,1,0:T(8,128)(2,1)} %pad_maximum_fusion.4), calls=%async_computation | async-start | bytes 2097152 | tf_op jit(solution)/shard_map/all_to_all | solution.py:65
  385.5 20.3 %collective-permute-start.22 = (bf16[128,1,128]{2,0,1:T(8,128)(2,1)}, bf16[128,1,128]{2,0,1:T(8,128)(2,1)}, u32[]{:S(2)}, u32[]{:S(2)}) collective-permute-start(bf16[128,1,128]{2,0,1:T(8,128)(2,1)} %get-tuple-element.492), channel_id=1, source_target_pairs={{0,2},{1,3},{2,0},{3,1},{4,6},{5,7},{6,4},{7,5},{8,10},{9,11},{10,... | collective-permute-start | bytes 98312 | tf_op jit(solution)/shard_map/ppermute | solution.py:51
  390.0 33.8 %collective-permute-start.26 = (bf16[2,2,128,128]{2,3,0,1:T(8,128)(2,1)}, bf16[2,2,128,128]{2,3,0,1:T(8,128)(2,1)S(1)}, u32[]{:S(2)}, u32[]{:S(2)}) collective-permute-start(bf16[2,2,128,128]{2,3,0,1:T(8,128)(2,1)} %convert_element_type.207), channel_id=1, source_target_pairs={{0,4},{4,0},{8,12},{12,8},{16,20},{20,16},{24,28},{28,24},{1,5},{5... | collective-permute-start | bytes 393224 | tf_op jit(solution)/shard_map/ppermute | solution.py:35
  391.7 24.1 %collective-permute-start.24 = (bf16[2,128,128]{2,1,0:T(8,128)(2,1)}, bf16[2,128,128]{2,1,0:T(8,128)(2,1)}, u32[]{:S(2)}, u32[]{:S(2)}) collective-permute-start(bf16[2,128,128]{2,1,0:T(8,128)(2,1)} %get-tuple-element.466), channel_id=1, source_target_pairs={{0,4},{4,8},{8,12},{12,16},{16,20},{20,24},{24,28},{1,5},{5,9},{9,... | collective-permute-start | bytes 196616 | tf_op jit(solution)/shard_map/ppermute | solution.py:17
  396.8 117.3 %all-to-all-start.9 = ((bf16[16,2,128,128]{3,2,1,0:T(8,128)(2,1)}), bf16[16,2,128,128]{3,2,1,0:T(8,128)(2,1)}, u32[]{:S(2)}, u32[]{:S(2)}) async-start(bf16[16,2,128,128]{3,2,1,0:T(8,128)(2,1)} %copy.524), calls=%async_computation.9 | async-start | bytes 2097152 | tf_op jit(solution)/shard_map/all_to_all | solution.py:251
  413.6 20.7 %collective-permute-start.8 = (bf16[128,8,128]{2,1,0:T(8,128)(2,1)S(1)}, bf16[128,8,128]{2,1,0:T(8,128)(2,1)}, u32[]{:S(2)}, u32[]{:S(2)}) collective-permute-start(bf16[128,8,128]{2,1,0:T(8,128)(2,1)S(1)} %copy-done.22), channel_id=1, source_target_pairs={{0,2},{1,3},{2,0},{3,1},{4,6},{5,7},{6,4},{7,5},{8,10},{9,11},{10,... | collective-permute-start | bytes 786440 | tf_op jit(solution)/shard_map/ppermute | solution.py:51
  415.8 21.5 %collective-permute-start.9 = (bf16[128,8,128]{2,1,0:T(8,128)(2,1)S(1)}, bf16[128,8,128]{2,1,0:T(8,128)(2,1)}, u32[]{:S(2)}, u32[]{:S(2)}) collective-permute-start(bf16[128,8,128]{2,1,0:T(8,128)(2,1)S(1)} %copy-done.21), channel_id=1, source_target_pairs={{0,3},{1,0},{2,1},{3,2},{4,7},{5,4},{6,5},{7,6},{8,11},{9,8},{10,9... | collective-permute-start | bytes 786440 | tf_op jit(solution)/shard_map/ppermute | solution.py:51
  418.6 33.2 %collective-permute-start.18 = (bf16[128,8,128]{2,1,0:T(8,128)(2,1)}, bf16[128,8,128]{2,1,0:T(8,128)(2,1)}, u32[]{:S(2)}, u32[]{:S(2)}) collective-permute-start(bf16[128,8,128]{2,1,0:T(8,128)(2,1)} %get-tuple-element.449), channel_id=1, source_target_pairs={{0,1},{1,2},{2,3},{3,0},{4,5},{5,6},{6,7},{7,4},{8,9},{9,10},{10,1... | collective-permute-start | bytes 786440 | tf_op jit(solution)/shard_map/ppermute | solution.py:51
  423.8 44.1 %collective-permute-start.19 = (bf16[128,8,128]{2,1,0:T(8,128)(2,1)}, bf16[128,8,128]{2,1,0:T(8,128)(2,1)S(1)}, u32[]{:S(2)}, u32[]{:S(2)}) collective-permute-start(bf16[128,8,128]{2,1,0:T(8,128)(2,1)} %get-tuple-element.448), channel_id=1, source_target_pairs={{0,2},{1,3},{2,0},{3,1},{4,6},{5,7},{6,4},{7,5},{8,10},{9,11},{10,... | collective-permute-start | bytes 786440 | tf_op jit(solution)/shard_map/ppermute | solution.py:51
  425.3 45.8 %collective-permute-start.20 = (bf16[128,8,128]{2,1,0:T(8,128)(2,1)S(1)}, bf16[128,8,128]{2,1,0:T(8,128)(2,1)S(1)}, u32[]{:S(2)}, u32[]{:S(2)}) collective-permute-start(bf16[128,8,128]{2,1,0:T(8,128)(2,1)S(1)} %get-tuple-element.447), channel_id=1, source_target_pairs={{0,3},{1,0},{2,1},{3,2},{4,7},{5,4},{6,5},{7,6},{8,11},{9,8},{10,9... | collective-permute-start | bytes 786440 | tf_op jit(solution)/shard_map/ppermute | solution.py:51
  434.3 48.5 %collective-permute-start.12 = (bf16[128,8,128]{2,1,0:T(8,128)(2,1)}, bf16[128,8,128]{2,1,0:T(8,128)(2,1)}, u32[]{:S(2)}, u32[]{:S(2)}) collective-permute-start(bf16[128,8,128]{2,1,0:T(8,128)(2,1)} %get-tuple-element.457), channel_id=1, source_target_pairs={{0,1},{1,2},{2,3},{3,0},{4,5},{5,6},{6,7},{7,4},{8,9},{9,10},{10,1... | collective-permute-start | bytes 786440 | tf_op jit(solution)/shard_map/ppermute | solution.py:51
  437.3 51.7 %collective-permute-start.13 = (bf16[128,8,128]{2,1,0:T(8,128)(2,1)}, bf16[128,8,128]{2,1,0:T(8,128)(2,1)}, u32[]{:S(2)}, u32[]{:S(2)}) collective-permute-start(bf16[128,8,128]{2,1,0:T(8,128)(2,1)} %get-tuple-element.456), channel_id=1, source_target_pairs={{0,2},{1,3},{2,0},{3,1},{4,6},{5,7},{6,4},{7,5},{8,10},{9,11},{10,... | collective-permute-start | bytes 786440 | tf_op jit(solution)/shard_map/ppermute | solution.py:51
  451.8 42.5 %collective-permute-start.14 = (bf16[128,8,128]{2,1,0:T(8,128)(2,1)}, bf16[128,8,128]{2,1,0:T(8,128)(2,1)}, u32[]{:S(2)}, u32[]{:S(2)}) collective-permute-start(bf16[128,8,128]{2,1,0:T(8,128)(2,1)} %get-tuple-element.455), channel_id=1, source_target_pairs={{0,3},{1,0},{2,1},{3,2},{4,7},{5,4},{6,5},{7,6},{8,11},{9,8},{10,9... | collective-permute-start | bytes 786440 | tf_op jit(solution)/shard_map/ppermute | solution.py:51
  467.9 30.7 %collective-permute-start.15 = (bf16[128,8,128]{2,1,0:T(8,128)(2,1)}, bf16[128,8,128]{2,1,0:T(8,128)(2,1)}, u32[]{:S(2)}, u32[]{:S(2)}) collective-permute-start(bf16[128,8,128]{2,1,0:T(8,128)(2,1)} %get-tuple-element.445), channel_id=1, source_target_pairs={{0,1},{1,2},{2,3},{3,0},{4,5},{5,6},{6,7},{7,4},{8,9},{9,10},{10,1... | collective-permute-start | bytes 786440 | tf_op jit(solution)/shard_map/ppermute | solution.py:51
  479.5 22.2 %collective-permute-start.16 = (bf16[128,8,128]{2,1,0:T(8,128)(2,1)}, bf16[128,8,128]{2,1,0:T(8,128)(2,1)}, u32[]{:S(2)}, u32[]{:S(2)}) collective-permute-start(bf16[128,8,128]{2,1,0:T(8,128)(2,1)} %get-tuple-element.444), channel_id=1, source_target_pairs={{0,2},{1,3},{2,0},{3,1},{4,6},{5,7},{6,4},{7,5},{8,10},{9,11},{10,... | collective-permute-start | bytes 786440 | tf_op jit(solution)/shard_map/ppermute | solution.py:51
  489.0 23.8 %collective-permute-start.28 = (bf16[2,2,128,128]{2,3,0,1:T(8,128)(2,1)}, bf16[2,2,128,128]{2,3,0,1:T(8,128)(2,1)}, u32[]{:S(2)}, u32[]{:S(2)}) collective-permute-start(bf16[2,2,128,128]{2,3,0,1:T(8,128)(2,1)} %fusion.100), channel_id=1, source_target_pairs={{0,16},{4,20},{8,24},{12,28},{16,0},{20,4},{24,8},{28,12},{1,17},{... | collective-permute-start | bytes 393224 | tf_op jit(solution)/shard_map/ppermute | solution.py:35
  (104 other events, 878.8 us)
Sparse Core Ops, SparseCore 0:
  31.8 26.8 all-gather.2
  61.1 27.9 all-gather.4
